TPU v7x, 32 devices: a whole 2x2x4 slice. The times are simulated.
32 devices in a mesh: seq: 8 (over z, y), fsdp: 4 (over x, core).
Axes of the slice: x: 2, y: 2, z: 4, core: 2. Of those that a mesh axis runs over, the one named last changes fastest.
Arguments:
- inputs: bfloat16 [12288, 1536], P(('seq', 'fsdp')), may hold values from -15 to 15
- layer_norm_gain: float32 [1536], replicated, may hold values from 0.25 to 1.75
- layer_norm_bias: float32 [1536], replicated, may hold values from -4 to 4
- w_in: bfloat16 [1536, 3072], P('fsdp'), may hold values from -0.15625 to 0.15625
- dw_kernel: float32 [32, 1536], replicated, may hold values from -1 to 1
- bn_gain: float32 [1536], replicated, may hold values from 0.25 to 1.75
- bn_bias: float32 [1536], replicated, may hold values from -4 to 4
- cotangent: bfloat16 [12288, 1536], P(('seq', 'fsdp')), may hold values from -6 to 6
Outputs:
- output: bfloat16 [12288, 1536], P(('seq', 'fsdp'))
- input_gradient: bfloat16 [12288, 1536], P(('seq', 'fsdp'))
- grad_w_in: float32 [1536, 3072], P('fsdp')
- grad_kernel: float32 [32, 1536], replicated
- grad_bn_gain: float32 [1536], replicated
- grad_bn_bias: float32 [1536], replicated
- layer_norm_gain_gradient: float32 [1536], replicated
- grad_ln_bias: float32 [1536], replicated
All inputs are finite; a program needn't handle non-finite values.
Results may differ from a plain program's by a relative error of at most 0.012.
The roundings to bfloat16 on the way count: a program that leaves them out, or rounds other values in their place, can miss the bound.
Values may be sent and summed in bfloat16 or wider, within the bound.
No kernel may reach another device: no remote copies, remote signals or barrier semaphores. Data moves between devices by JAX's collectives and lax.ppermute only.
A program may use at most 128 MiB of HBM per device.

v0:
```python
import jax
import jax.numpy as jnp
from jax import lax
from jax.sharding import PartitionSpec as P

epsilon = 1e-05


def from_behind(block, axis, distance):
    devices = range(lax.axis_size(axis))
    route = [(i - distance, i) for i in devices if i - distance in devices]
    return lax.ppermute(block, axis, route)


def tree_sum(tree, axis):
    count = lax.axis_size(axis)
    if count & count - 1:
        return lax.psum(tree, axis)
    stride = 1
    while stride < count:
        route = [(i, i ^ stride) for i in range(count)]
        tree = jax.tree.map(lambda x: x + lax.ppermute(x, axis, route), tree)
        stride *= 2
    return tree


def on_device(
    inputs, layer_norm_gain, layer_norm_bias, w_in, dw_kernel, bn_gain, bn_bias, cotangent
):
    tok_rows = inputs.shape[0]
    features = inputs.shape[1]
    kernel_len = dw_kernel.shape[0]
    all_frames = tok_rows * lax.axis_size("seq") * lax.axis_size("fsdp")
    frames = inputs.astype(jnp.float32)
    row_mean = jnp.mean(frames, axis=-1, keepdims=True)
    centered_rows = frames - row_mean
    row_inverse_deviation = lax.rsqrt(
        jnp.mean(centered_rows * centered_rows, axis=-1, keepdims=True) + epsilon
    )
    standardized_input = centered_rows * row_inverse_deviation
    normalized_rows = (standardized_input * layer_norm_gain + layer_norm_bias).astype(jnp.bfloat16)
    full_weight = lax.all_gather(w_in, "fsdp", axis=0, tiled=True)
    hidden = jnp.dot(normalized_rows, full_weight, preferred_element_type=jnp.float32)
    value_part = hidden[:, :features]
    gate_sig = jax.nn.sigmoid(hidden[:, features:])
    glu = (value_part * gate_sig).astype(jnp.bfloat16)
    past_rim = from_behind(glu[tok_rows - (kernel_len - 1) :], ("seq", "fsdp"), 1)
    padded_glu = jnp.concatenate([past_rim, glu], axis=0).astype(jnp.float32)
    conv_out = jnp.zeros((tok_rows, features), jnp.float32)
    for offset in range(kernel_len):
        conv_out = (
            conv_out
            + dw_kernel[offset]
            * padded_glu[kernel_len - 1 - offset : kernel_len - 1 - offset + tok_rows]
        )
    chan_mean = tree_sum(jnp.sum(conv_out, axis=0), ("seq", "fsdp")) / all_frames
    conv_centred = conv_out - chan_mean
    chan_var = tree_sum(jnp.sum(conv_centred * conv_centred, axis=0), ("seq", "fsdp")) / all_frames
    bn_rstd = lax.rsqrt(chan_var + epsilon)
    chat = conv_centred * bn_rstd
    z_value = chat * bn_gain + bn_bias
    z_sig = jax.nn.sigmoid(z_value)
    output = (z_value * z_sig).astype(jnp.bfloat16)
    grad_z = cotangent.astype(jnp.float32) * z_sig * (1.0 + z_value * (1.0 - z_sig))
    grad_bn_bias, grad_bn_gain = tree_sum(
        (jnp.sum(grad_z, axis=0), jnp.sum(grad_z * chat, axis=0)), ("seq", "fsdp")
    )
    grad_conv = (
        bn_gain * bn_rstd * (grad_z - grad_bn_bias / all_frames - chat * grad_bn_gain / all_frames)
    )
    future_rim = from_behind(grad_conv[: kernel_len - 1], ("seq", "fsdp"), -1)
    padded_grad = jnp.concatenate([grad_conv, future_rim], axis=0)
    grad_glu = jnp.zeros((tok_rows, features), jnp.float32)
    kernel_rows = []
    for offset in range(kernel_len):
        grad_glu = grad_glu + dw_kernel[offset] * padded_grad[offset : offset + tok_rows]
        kernel_rows.append(
            jnp.sum(
                grad_conv
                * padded_glu[kernel_len - 1 - offset : kernel_len - 1 - offset + tok_rows],
                axis=0,
            )
        )
    kernel_portion = jnp.stack(kernel_rows, axis=0)
    grad_value = grad_glu * gate_sig
    grad_gate = grad_glu * value_part * gate_sig * (1.0 - gate_sig)
    grad_hidden = jnp.concatenate([grad_value, grad_gate], axis=1).astype(jnp.bfloat16)
    normalized_gradient = lax.dot_general(
        grad_hidden, full_weight, (((1,), (1,)), ((), ())), preferred_element_type=jnp.float32
    )
    grad_kernel, layer_norm_gain_gradient, grad_ln_bias = tree_sum(
        (
            kernel_portion,
            jnp.sum(normalized_gradient * standardized_input, axis=0),
            jnp.sum(normalized_gradient, axis=0),
        ),
        ("seq", "fsdp"),
    )
    rescaled_rows = normalized_gradient * layer_norm_gain
    input_gradient = row_inverse_deviation * (
        rescaled_rows
        - jnp.mean(rescaled_rows, axis=-1, keepdims=True)
        - standardized_input * jnp.mean(rescaled_rows * standardized_input, axis=-1, keepdims=True)
    )
    row_share = lax.psum_scatter(
        lax.dot_general(
            normalized_rows,
            grad_hidden,
            (((0,), (0,)), ((), ())),
            preferred_element_type=jnp.float32,
        ),
        "fsdp",
        scatter_dimension=0,
        tiled=True,
    )
    grad_w_in = lax.psum(row_share, "seq")
    return (
        output,
        input_gradient.astype(jnp.bfloat16),
        grad_w_in,
        grad_kernel,
        grad_bn_gain,
        grad_bn_bias,
        layer_norm_gain_gradient,
        grad_ln_bias,
    )


def solution(mesh):
    placed = (
        P(("seq", "fsdp"), None),
        P(),
        P(),
        P("fsdp", None),
        P(),
        P(),
        P(),
        P(("seq", "fsdp"), None),
    )
    return jax.shard_map(
        on_device,
        mesh=mesh,
        in_specs=placed,
        out_specs=(
            P(("seq", "fsdp"), None),
            P(("seq", "fsdp"), None),
            P("fsdp", None),
            P(),
            P(),
            P(),
            P(),
            P(),
        ),
        check_vma=False,
    )
```

profile of v0, /device:TPU:0, one launch (start us, length us, event | category | flops | bytes accessed | tf_op | source)
XLA Modules:
  0.0 560.9 jit_solution(14859436354774125420)
XLA Ops:
  9.3 67.3 %all-gather.2.cloned.1.call-done = bf16[1536,3072]{1,0:T(8,128)(2,1)} async-done(((bf16[384,3072]{1,0:T(8,128)(2,1)}), bf16[1536,3072]{1,0:T(8,128)(2,1)}) %all-gather.2.cloned.1.call-update) | async-done | bytes 9437200 | tf_op jit(solution)/shard_map/all_gather | solution.py:42
  76.6 6.7 %fusion.114 = f32[384,3072]{1,0:T(8,128)S(1)} fusion(bf16[1536,3072]{1,0:T(8,128)(2,1)} %all-gather.2.cloned.1.call-done, bf16[384,1536]{1,0:T(8,128)(2,1)S(1)} %copy-done.2, f32[1536]{0:T(1024)S(1)} %copy-done.10, f32[1536]{0:T(1024)S(1)} %copy-done.9, f32[384]{0:T(512)S(1)} %add_rsqrt_fusion.1, f32[384]{0:T(512)S(1)} %broadcast_multiply_fusion.3), kind=kOutput, calls=%fused_computation.258 | convolution fusion | flops 3627417600 | bytes 15350784 | tf_op jit(solution)/shard_map/dot_general | solution.py:43
  83.9 1.5 copy-done
  85.5 2.2 collective-permute-start
  88.9 9.4 %fusion.119 = (f32[1536]{0:T(1024)S(1)}, f32[384,1536]{1,0:T(8,128)S(1)}) fusion(f32[415,1536]{1,0:T(8,128)S(1)} %maximum_convert_fusion, f32[1536]{0:T(1024)S(1)} %get-tuple-element.76, f32[1536]{0:T(1024)S(1)} %get-tuple-element.77, f32[1536]{0:T(1024)S(1)} %get-tuple-element.47, f32[1536]{0:T(1024)S(1)} %get-tuple-element.48, ...), kind=kLoop, calls=%fused_computation.261 | loop fusion | flops 37747200 | bytes 78059520 | tf_op jit(solution)/shard_map/reduce_sum | solution.py:56
  100.2 2.6 collective-permute-start.2
  102.8 1.6 collective-permute-done.2
  104.4 4.1 collective-permute-start.3
  108.5 1.6 collective-permute-done.3
  110.2 2.9 collective-permute-start.4
  113.1 1.6 collective-permute-done.4
  114.7 2.9 collective-permute-start.5
  117.7 1.6 collective-permute-done.5
  120.8 3.6 collective-permute-done.7
  125.6 2.6 collective-permute-done.8
  128.1 2.0 collective-permute-start.9
  130.1 1.6 collective-permute-done.9
  131.8 2.9 collective-permute-start.10
  134.7 1.6 collective-permute-done.10
  136.4 2.5 fusion.116
  140.2 1.9 collective-permute-start.17
  142.1 1.6 collective-permute-done.12
  145.7 1.6 collective-permute-done.13
  147.4 2.0 collective-permute-start.14
  151.0 2.9 collective-permute-start.15
  153.9 1.6 collective-permute-start.20
  156.2 2.3 collective-permute-done.20
  158.5 7.1 %multiply_reduce_fusion = (f32[1536]{0:T(1024)S(1)}, f32[1536]{0:T(1024)S(1)}, f32[1536]{0:T(1024)S(1)}, f32[1536]{0:T(1024)S(1)}, f32[1536]{0:T(1024)S(1)}, /*i...) fusion(f32[415,1536]{1,0:T(8,128)S(1)} %maximum_convert_fusion,, ...), kind=kLoop, calls=%fused_computation.169 | loop fusion | flops 31822848 | bytes 48519168 | tf_op jit(solution)/shard_map/reduce_sum | solution.py:78
  168.5 1.9 collective-permute-done.21
  170.3 40.4 %multiply_convert_fusion.1 = (bf16[384,1536]{1,0:T(8,128)(2,1)S(1)}, f32[384,1536]{1,0:T(8,128)}) fusion(f32[384,3072]{1,0:T(8,128)} %copy-done, f32[31,1536]{1,0:T(8,128)S(1)} %collective-permute-done.21, f32[384,1536]{1,0:T(8,128)} %copy-done.1, f32[1536]{0:T(1024)S(1)} %get-tuple-element.76, f32[1536]{0:T(1024)S(1)} %get-tuple-element.77, ...), kind=kLoop, calls=%fused_computation.202 | loop fusion | flops 58392576 | bytes 8644608 | tf_op jit(solution)/shard_map/convert
  210.8 4.4 multiply_convert_fusion
  216.3 9.4 %fusion.109 = f32[1536,3072]{1,0:T(8,128)} fusion(bf16[384,1536]{1,0:T(8,128)(2,1)S(1)} %multiply_convert_fusion, bf16[384,1536]{1,0:T(8,128)(2,1)S(1)} %get-tuple-element.79, bf16[384,1536]{1,0:T(8,128)(2,1)S(1)} %copy-done.3, f32[1536]{0:T(1024)S(1)} %copy-done.10, f32[1536]{0:T(1024)S(1)} %copy-done.9, f32[384]{0:T(512)S(1)} %add_rsqrt_fusion.1, ...), kind=kOutput, calls=%fused_computation.214 | convolution fusion | flops 3632136192 | bytes 22428672 | tf_op jit(solution)/shard_map/dot_general | solution.py:106
  226.0 140.8 %reduce-scatter.2.cloned.1.call-done = f32[384,3072]{1,0:T(8,128)} async-done(((f32[1536,3072]{1,0:T(8,128)}), f32[384,3072]{1,0:T(8,128)}) %reduce-scatter.2.cloned.1.call-update) | async-done | bytes 4718608 | tf_op jit(solution)/shard_map/reduce_scatter | solution.py:105
  366.8 5.4 multiply_reduce_fusion.18
  374.9 6.6 %collective-permute-done.23 = f32[32,1536]{1,0:T(8,128)S(1)} collective-permute-done((f32[32,1536]{1,0:T(8,128)S(1)}, f32[32,1536]{1,0:T(8,128)S(1)}, u32[]{:S(2)}, u32[]{:S(2)}) %collective-permute-start.23) | collective-permute-done | bytes 196640 | tf_op jit(solution)/shard_map/ppermute | solution.py:22
  381.6 1.5 collective-permute-start.24
  383.1 9.1 %fusion.12 = (f32[1536]{0:T(1024)S(1)}, f32[384]{0:T(512)S(1)}, f32[384]{0:T(512)S(1)}, f32[1536]{0:T(1024)S(1)}, f32[384,1536]{1,0:T(8,128)S(1)}) fusion(bf16[384,1536]{1,0:T(8,128)(2,1)} %param.8, f32[384]{0:T(512)S(1)} %add_rsqrt_fusion.1, f32[384]{0:T(512)S(1)} %broadcast_multiply_fusion.3, f32[1536]{0:T(1024)S(1)} %copy-done.9, ...), kind=kOutput, calls=%fused_computation.44 | convolution fusion | flops 3634491392 | bytes 15360000 | tf_op jit(solution)/shard_map/dot_general | solution.py:88
  395.5 1.6 collective-permute-done.28
  399.2 1.6 collective-permute-done.29
  400.8 1.5 collective-permute-start.30
  402.9 1.5 collective-permute-start.25
  404.4 2.2 collective-permute-done.30
  407.1 2.4 collective-permute-start.36
  409.5 17.2 %collective-permute-done.25 = f32[32,1536]{1,0:T(8,128)S(1)} collective-permute-done((f32[32,1536]{1,0:T(8,128)S(1)}, f32[32,1536]{1,0:T(8,128)S(1)}, u32[]{:S(2)}, u32[]{:S(2)}) %collective-permute-start.25) | collective-permute-done | bytes 196640 | tf_op jit(solution)/shard_map/ppermute | solution.py:22
  427.3 1.8 fusion.11
  430.3 9.8 %collective-permute-done.26 = f32[32,1536]{1,0:T(8,128)S(1)} collective-permute-done((f32[32,1536]{1,0:T(8,128)S(1)}, f32[32,1536]{1,0:T(8,128)S(1)}, u32[]{:S(2)}, u32[]{:S(2)}) %collective-permute-start.26) | collective-permute-done | bytes 196640 | tf_op jit(solution)/shard_map/ppermute | solution.py:22
  440.8 108.5 %all-reduce.2.cloned.1.call-done = f32[384,3072]{1,0:T(8,128)} async-done(((f32[384,3072]{1,0:T(8,128)}), f32[384,3072]{1,0:T(8,128)}) %all-reduce.2.cloned.1.call-update) | async-done | bytes 4718608 | tf_op jit(solution)/shard_map/psum | solution.py:116
  549.3 5.1 copy.17
  (154 shorter events, 29.6 us)
Async XLA Ops:
  7.2 69.4 %copy-start.9 = (f32[1536]{0:T(1024)S(1)}, f32[1536]{0:T(1024)}, u32[]{:S(2)}) copy-start(f32[1536]{0:T(1024)} %param.9) | copy-start | bytes 18436
  7.2 69.4 %copy-start.10 = (f32[1536]{0:T(1024)S(1)}, f32[1536]{0:T(1024)}, u32[]{:S(2)}) copy-start(f32[1536]{0:T(1024)} %param.10) | copy-start | bytes 18436
  7.2 69.4 %all-gather.2.cloned.1.call-start = ((), (), s32[]{:S(2)}) async-start(), calls=%async_computation.1 | async-start | bytes 11796480 | tf_op jit(solution)/shard_map/all_gather | solution.py:42
  7.9 358.8 %reduce-scatter.2.cloned.1.call-start = ((), (), s32[]{:S(2)}) async-start(), calls=%async_computation.2 | async-start | bytes 23592960 | tf_op jit(solution)/shard_map/reduce_scatter | solution.py:105
  85.5 3.1 collective-permute-start
  98.4 38.0 %copy-start.11 = (f32[1536]{0:T(1024)S(1)}, f32[1536]{0:T(1024)}, u32[]{:S(2)}) copy-start(f32[1536]{0:T(1024)} %param.13) | copy-start | bytes 18436
  98.4 38.0 %copy-start.5 = (bf16[384,1536]{1,0:T(8,128)(2,1)S(1)}, bf16[384,1536]{1,0:T(8,128)(2,1)}, u32[]{:S(2)}) copy-start(bf16[384,1536]{1,0:T(8,128)(2,1)} %param.15) | copy-start | bytes 3538948
  98.4 38.0 %copy-start.12 = (f32[1536]{0:T(1024)S(1)}, f32[1536]{0:T(1024)}, u32[]{:S(2)}) copy-start(f32[1536]{0:T(1024)} %param.14) | copy-start | bytes 18436
  98.4 1.8 collective-permute-start.1
  100.2 4.3 collective-permute-start.2
  104.4 5.7 %collective-permute-start.3 = (f32[1536]{0:T(1024)S(1)}, f32[1536]{0:T(1024)S(1)}, u32[]{:S(2)}, u32[]{:S(2)}) collective-permute-start(f32[1536]{0:T(1024)S(1)} %add.374), channel_id=1, source_target_pairs={{0,4},{1,5},{2,6},{3,7},{4,0},{5,1},{6,2},{7,3},{8,12},{9,13},{10,... | collective-permute-start | bytes 18440 | tf_op jit(solution)/shard_map/ppermute | solution.py:22
  110.2 4.6 collective-permute-start.4
  114.7 4.6 collective-permute-start.5
  119.6 1.2 collective-permute-start.6
  120.8 3.7 collective-permute-start.7
  124.5 3.7 collective-permute-start.8
  128.1 3.7 collective-permute-start.9
  131.8 4.6 collective-permute-start.10
  138.9 1.2 collective-permute-start.11
  138.9 1.3 collective-permute-start.16
  140.0 3.7 collective-permute-start.12
  140.2 4.6 collective-permute-start.17
  143.7 3.7 collective-permute-start.13
  144.8 4.6 collective-permute-start.18
  147.4 3.7 collective-permute-start.14
  149.4 4.6 collective-permute-start.19
  151.0 4.5 collective-permute-start.15
  153.9 4.6 collective-permute-start.20
  158.5 7.1 %copy-start.13 = (f32[1536]{0:T(1024)}, f32[1536]{0:T(1024)S(1)}, u32[]{:S(2)}) copy-start(f32[1536]{0:T(1024)S(1)} %add.398) | copy-start | bytes 18436
  167.0 3.3 collective-permute-start.21
  210.8 5.5 copy-start.3
  225.7 323.6 %all-reduce.2.cloned.1.call-start = ((), (), s32[]{:S(2)}) async-start(), calls=%async_computation.3 | async-start | bytes 9437184 | tf_op jit(solution)/shard_map/psum | solution.py:116
  373.0 1.5 collective-permute-start.22
  374.6 7.0 %collective-permute-start.23 = (f32[32,1536]{1,0:T(8,128)S(1)}, f32[32,1536]{1,0:T(8,128)S(1)}, u32[]{:S(2)}, u32[]{:S(2)}) collective-permute-start(f32[32,1536]{1,0:T(8,128)S(1)} %add.430), channel_id=1, source_target_pairs={{0,2},{1,3},{2,0},{3,1},{4,6},{5,7},{6,4},{7,5},{8,10},{9,11},{10,... | collective-permute-start | bytes 589832 | tf_op jit(solution)/shard_map/ppermute | solution.py:22
  381.6 45.7 %copy-start.4 = (bf16[384,1536]{1,0:T(8,128)(2,1)S(1)}, bf16[384,1536]{1,0:T(8,128)(2,1)}, u32[]{:S(2)}) copy-start(bf16[384,1536]{1,0:T(8,128)(2,1)} %param.8) | copy-start | bytes 3538948
  381.6 21.3 %collective-permute-start.24 = (f32[32,1536]{1,0:T(8,128)S(1)}, f32[32,1536]{1,0:T(8,128)S(1)}, u32[]{:S(2)}, u32[]{:S(2)}) collective-permute-start(f32[32,1536]{1,0:T(8,128)S(1)} %add.431), channel_id=1, source_target_pairs={{0,4},{1,5},{2,6},{3,7},{4,0},{5,1},{6,2},{7,3},{8,12},{9,13},{10,... | collective-permute-start | bytes 589832 | tf_op jit(solution)/shard_map/ppermute | solution.py:22
  392.2 1.2 collective-permute-start.27
  392.3 1.7 collective-permute-start.32
  393.5 3.7 collective-permute-start.28
  394.0 3.7 collective-permute-start.33
  397.1 3.7 collective-permute-start.29
  397.7 4.6 collective-permute-start.34
  400.8 5.8 %collective-permute-start.30 = (f32[1536]{0:T(1024)S(1)}, f32[1536]{0:T(1024)S(1)}, u32[]{:S(2)}, u32[]{:S(2)}) collective-permute-start(f32[1536]{0:T(1024)S(1)} %add.437), channel_id=1, source_target_pairs={{0,8},{1,9},{2,10},{3,11},{4,12},{5,13},{6,14},{7,15},{8,0},{9,1},... | collective-permute-start | bytes 18440 | tf_op jit(solution)/shard_map/ppermute | solution.py:22
  402.3 4.8 collective-permute-start.35
  402.9 23.9 %collective-permute-start.25 = (f32[32,1536]{1,0:T(8,128)S(1)}, f32[32,1536]{1,0:T(8,128)S(1)}, u32[]{:S(2)}, u32[]{:S(2)}) collective-permute-start(f32[32,1536]{1,0:T(8,128)S(1)} %add.432), channel_id=1, source_target_pairs={{0,8},{1,9},{2,10},{3,11},{4,12},{5,13},{6,14},{7,15},{8,0},{9,1},... | collective-permute-start | bytes 589832 | tf_op jit(solution)/shard_map/ppermute | solution.py:22
  406.6 22.5 %collective-permute-start.31 = (f32[1536]{0:T(1024)S(1)}, f32[1536]{0:T(1024)S(1)}, u32[]{:S(2)}, u32[]{:S(2)}) collective-permute-start(f32[1536]{0:T(1024)S(1)} %add.438), channel_id=1, source_target_pairs={{0,16},{1,17},{2,18},{3,19},{4,20},{5,21},{6,22},{7,23},{8,24},{9,... | collective-permute-start | bytes 18440 | tf_op jit(solution)/shard_map/ppermute | solution.py:22
  407.1 22.6 %collective-permute-start.36 = (f32[1536]{0:T(1024)S(1)}, f32[1536]{0:T(1024)S(1)}, u32[]{:S(2)}, u32[]{:S(2)}) collective-permute-start(f32[1536]{0:T(1024)S(1)} %add.443), channel_id=1, source_target_pairs={{0,16},{1,17},{2,18},{3,19},{4,20},{5,21},{6,22},{7,23},{8,24},{9,... | collective-permute-start | bytes 18440 | tf_op jit(solution)/shard_map/ppermute | solution.py:22
  426.8 13.4 %collective-permute-start.26 = (f32[32,1536]{1,0:T(8,128)S(1)}, f32[32,1536]{1,0:T(8,128)S(1)}, u32[]{:S(2)}, u32[]{:S(2)}) collective-permute-start(f32[32,1536]{1,0:T(8,128)S(1)} %add.433), channel_id=1, source_target_pairs={{0,16},{1,17},{2,18},{3,19},{4,20},{5,21},{6,22},{7,23},{8,24},{9,... | collective-permute-start | bytes 589832 | tf_op jit(solution)/shard_map/ppermute | solution.py:22
  (6 other events, 11.4 us)
Sparse Core Ops, SparseCore 0:
  9.6 66.9 all-gather.1
  225.8 140.8 reduce-scatter.1
  370.8 178.4 all-reduce.1
where the time goes:
time: 561 us
  waiting for transfers between devices  387 us (69%)
  other arithmetic  75.8 us (14%)
  starting transfers between devices  48.7 us (9%)
  matrix products  25.2 us (4%)
  between operations  14.3 us (3%)
  local copies, waits for them, and re-layouts  10.4 us (2%)
    reduce_scatter x1, waiting for transfers between devices, on_device(): lax.psum_scatter(lax.dot_general(normalized_rows, grad_hidden, (((0,), (0...  141 us
    psum x1, waiting for transfers between devices, on_device(): grad_w_in = lax.psum(row_share, 'seq')  109 us
    all_gather x1, waiting for transfers between devices, on_device(): full_weight = lax.all_gather(w_in, 'fsdp', axis=0, tiled=True)  67.3 us
    ppermute x35, waiting for transfers between devices, tree_sum(): tree = jax.tree.map(lambda x: x + lax.ppermute(x, axis, route), tree)  66.7 us
    another operation x2, other arithmetic  44.9 us
    ppermute x35, starting transfers between devices, tree_sum(): tree = jax.tree.map(lambda x: x + lax.ppermute(x, axis, route), tree)  44.7 us
    reduce_sum x2, other arithmetic, on_device(): jnp.sum(grad_conv * padded_glu[kernel_len - 1 - offset:kernel_len - 1 - o...  12.6 us
  transfers between devices with their start and end apart: 40, of which 30 were waited for; matrix products, arithmetic and copies ran while one was open for 4% of the time, Pallas kernels for 0%

commit v1 on v0

--- a/solution.py
+++ b/solution.py
@@ -113,7 +113,7 @@
         scatter_dimension=0,
         tiled=True,
     )
-    grad_w_in = lax.psum(row_share, "seq")
+    grad_w_in = jnp.sum(lax.all_gather(row_share, "seq"), axis=0)
     return (
         output,
         input_gradient.astype(jnp.bfloat16),

time: 561 us -> 1110 us (1.98)
  waiting for transfers between devices: 387 us -> 929 us
  other arithmetic: 75.8 us -> 94.6 us
    all_gather x0 -> x1, waiting for transfers between devices: none -> 625 us  [on_device(): grad_w_in = jnp.sum(lax.all_gather(row_share, 'seq'), axis=0)]
    psum x1 -> x0, waiting for transfers between devices: 109 us -> none  [on_device(): grad_w_in = lax.psum(row_share, 'seq')]
    ppermute x35, waiting for transfers between devices: 66.7 us -> 92.6 us  [tree_sum(): tree = jax.tree.map(lambda x: x + lax.ppermute(x, axis, route), tree)]
    reduce_sum x0 -> x1, other arithmetic: none -> 16.5 us  [on_device(): grad_w_in = jnp.sum(lax.all_gather(row_share, 'seq'), axis=0)]
  transfers between devices with their start and end apart: 40 -> 40, of which waited for: 30 -> 32; matrix products, arithmetic and copies ran while one was open for 4% -> 2% of each run, Pallas kernels for 0% -> 0%
where the time goes in v1:
time: 1110 us
  waiting for transfers between devices  929 us (84%)
  other arithmetic  94.6 us (9%)
  starting transfers between devices  46.4 us (4%)
  matrix products  24.9 us (2%)
  between operations  14.3 us (1%)
    all_gather x1, waiting for transfers between devices, on_device(): grad_w_in = jnp.sum(lax.all_gather(row_share, 'seq'), axis=0)  625 us
    reduce_scatter x1, waiting for transfers between devices, on_device(): lax.psum_scatter(lax.dot_general(normalized_rows, grad_hidden, (((0,), (0...  141 us
    ppermute x35, waiting for transfers between devices, tree_sum(): tree = jax.tree.map(lambda x: x + lax.ppermute(x, axis, route), tree)  92.6 us
    all_gather x1, waiting for transfers between devices, on_device(): full_weight = lax.all_gather(w_in, 'fsdp', axis=0, tiled=True)  67.3 us
    another operation x2, other arithmetic  47.3 us
    ppermute x35, starting transfers between devices, tree_sum(): tree = jax.tree.map(lambda x: x + lax.ppermute(x, axis, route), tree)  42.4 us
  transfers between devices with their start and end apart: 40, of which 32 were waited for; matrix products, arithmetic and copies ran while one was open for 2% of the time, Pallas kernels for 0%

profile of v1, /device:TPU:0, one launch (start us, length us, event | category | flops | bytes accessed | tf_op | source)
XLA Modules:
  0.0 1114.6 jit_solution(17884948880873882363)
XLA Ops:
  9.3 67.3 %all-gather.4.cloned.1.call-done = bf16[1536,3072]{1,0:T(8,128)(2,1)} async-done(((bf16[384,3072]{1,0:T(8,128)(2,1)}), bf16[1536,3072]{1,0:T(8,128)(2,1)}) %all-gather.4.cloned.1.call-update) | async-done | bytes 9437200 | tf_op jit(solution)/shard_map/all_gather | solution.py:42
  76.6 6.5 fusion.114
  83.7 1.5 copy-done
  85.3 2.2 collective-permute-start
  88.7 9.4 fusion.119
  100.0 2.6 collective-permute-start.2
  102.6 1.6 collective-permute-done.2
  104.2 4.1 collective-permute-start.3
  108.3 1.6 collective-permute-done.3
  109.9 2.9 collective-permute-start.4
  112.9 1.6 collective-permute-done.4
  114.5 2.9 collective-permute-start.5
  117.5 1.6 collective-permute-done.5
  120.6 3.6 collective-permute-done.7
  125.4 2.6 collective-permute-done.8
  127.9 2.0 collective-permute-start.9
  129.9 1.6 collective-permute-done.9
  131.6 2.9 collective-permute-start.10
  134.5 1.6 collective-permute-done.10
  136.2 2.5 fusion.116
  140.0 1.9 collective-permute-start.17
  141.9 1.6 collective-permute-done.12
  145.5 1.6 collective-permute-done.13
  147.1 2.0 collective-permute-start.14
  150.8 2.9 collective-permute-start.15
  153.7 1.6 collective-permute-start.20
  155.9 2.3 collective-permute-done.20
  158.3 7.1 multiply_reduce_fusion
  166.8 1.5 collective-permute-start.21
  168.3 1.9 collective-permute-done.21
  170.2 42.9 %multiply_convert_fusion.1 = (bf16[384,1536]{1,0:T(8,128)(2,1)S(1)}, f32[384,1536]{1,0:T(8,128)}) fusion(f32[384,3072]{1,0:T(8,128)} %copy-done, f32[31,1536]{1,0:T(8,128)S(1)} %collective-permute-done.21, f32[384,1536]{1,0:T(8,128)} %copy-done.1, f32[1536]{0:T(1024)S(1)} %get-tuple-element.76, f32[1536]{0:T(1024)S(1)} %get-tuple-element.77, ...), kind=kLoop, calls=%fused_computation.202 | loop fusion | flops 58392576 | bytes 8644608 | tf_op jit(solution)/shard_map/convert
  213.1 4.4 multiply_convert_fusion
  218.5 9.4 fusion.109
  228.2 140.8 %reduce-scatter.2.cloned.1.call-done = f32[384,3072]{1,0:T(8,128)} async-done(((f32[1536,3072]{1,0:T(8,128)}), f32[384,3072]{1,0:T(8,128)}) %reduce-scatter.2.cloned.1.call-update) | async-done | bytes 4718608 | tf_op jit(solution)/shard_map/reduce_scatter | solution.py:105
  369.0 5.4 multiply_reduce_fusion.18
  377.2 6.6 collective-permute-done.23
  383.8 1.5 collective-permute-start.24
  385.4 9.0 fusion.12
  396.2 1.5 collective-permute-start.33
  397.7 1.6 collective-permute-done.28
  401.3 39.4 %collective-permute-done.29 = f32[1536]{0:T(1024)S(1)} collective-permute-done((f32[1536]{0:T(1024)S(1)}, f32[1536]{0:T(1024)S(1)}, u32[]{:S(2)}, u32[]{:S(2)}) %collective-permute-start.29) | collective-permute-done | bytes 6176 | tf_op jit(solution)/shard_map/ppermute | solution.py:22
  441.1 1.7 collective-permute-start.35
  444.8 2.6 collective-permute-start.36
  447.3 3.1 collective-permute-done.25
  450.6 1.8 fusion.11
  453.6 12.4 %collective-permute-done.26 = f32[32,1536]{1,0:T(8,128)S(1)} collective-permute-done((f32[32,1536]{1,0:T(8,128)S(1)}, f32[32,1536]{1,0:T(8,128)S(1)}, u32[]{:S(2)}, u32[]{:S(2)}) %collective-permute-start.26) | collective-permute-done | bytes 196640 | tf_op jit(solution)/shard_map/ppermute | solution.py:22
  466.6 624.9 %all-gather.6.cloned.1.call-done = f32[3072,3072]{1,0:T(8,128)} async-done(((f32[384,3072]{1,0:T(8,128)}), f32[3072,3072]{1,0:T(8,128)}) %all-gather.6.cloned.1.call-update) | async-done | bytes 37748752 | tf_op jit(solution)/shard_map/all_gather | solution.py:116
  1091.6 16.5 %reduce_sum.395 = f32[384,3072]{1,0:T(8,128)} reduce(f32[8,384,3072]{2,1,0:T(8,128)} %bitcast.3, f32[]{:T(128)} %constant.15.clone.1), dimensions={0}, to_apply=%region_9.0 | reduce | flops 8257536 | bytes 42467332 | tf_op jit(solution)/shard_map/reduce_sum | solution.py:116
  (154 shorter events, 27.4 us)
Async XLA Ops:
  7.2 69.4 %copy-start.9 = (f32[1536]{0:T(1024)S(1)}, f32[1536]{0:T(1024)}, u32[]{:S(2)}) copy-start(f32[1536]{0:T(1024)} %param.9) | copy-start | bytes 18436
  7.2 69.4 %copy-start.10 = (f32[1536]{0:T(1024)S(1)}, f32[1536]{0:T(1024)}, u32[]{:S(2)}) copy-start(f32[1536]{0:T(1024)} %param.10) | copy-start | bytes 18436
  7.2 69.4 %all-gather.4.cloned.1.call-start = ((), (), s32[]{:S(2)}) async-start(), calls=%async_computation.1 | async-start | bytes 11796480 | tf_op jit(solution)/shard_map/all_gather | solution.py:42
  7.9 361.0 %reduce-scatter.2.cloned.1.call-start = ((), (), s32[]{:S(2)}) async-start(), calls=%async_computation.2 | async-start | bytes 23592960 | tf_op jit(solution)/shard_map/reduce_scatter | solution.py:105
  85.3 3.1 collective-permute-start
  98.2 38.0 %copy-start.11 = (f32[1536]{0:T(1024)S(1)}, f32[1536]{0:T(1024)}, u32[]{:S(2)}) copy-start(f32[1536]{0:T(1024)} %param.13) | copy-start | bytes 18436
  98.2 38.0 %copy-start.5 = (bf16[384,1536]{1,0:T(8,128)(2,1)S(1)}, bf16[384,1536]{1,0:T(8,128)(2,1)}, u32[]{:S(2)}) copy-start(bf16[384,1536]{1,0:T(8,128)(2,1)} %param.15) | copy-start | bytes 3538948
  98.2 38.0 %copy-start.12 = (f32[1536]{0:T(1024)S(1)}, f32[1536]{0:T(1024)}, u32[]{:S(2)}) copy-start(f32[1536]{0:T(1024)} %param.14) | copy-start | bytes 18436
  98.2 1.8 collective-permute-start.1
  100.0 4.3 collective-permute-start.2
  104.2 5.7 collective-permute-start.3
  109.9 4.6 collective-permute-start.4
  114.5 4.6 collective-permute-start.5
  119.4 1.2 collective-permute-start.6
  120.6 3.7 collective-permute-start.7
  124.3 3.7 collective-permute-start.8
  127.9 3.7 collective-permute-start.9
  131.6 4.5 collective-permute-start.10
  138.6 1.2 collective-permute-start.11
  138.7 1.3 collective-permute-start.16
  139.8 3.7 collective-permute-start.12
  140.0 4.6 collective-permute-start.17
  143.5 3.7 collective-permute-start.13
  144.6 4.6 collective-permute-start.18
  147.1 3.7 collective-permute-start.14
  149.1 4.6 collective-permute-start.19
  150.8 4.5 collective-permute-start.15
  153.7 4.6 collective-permute-start.20
  158.3 7.1 copy-start.13
  166.8 3.3 collective-permute-start.21
  213.0 5.5 copy-start.3
  227.9 863.6 %all-gather.6.cloned.1.call-start = ((), (), s32[]{:S(2)}) async-start(), calls=%async_computation.3 | async-start | bytes 42467328 | tf_op jit(solution)/shard_map/all_gather | solution.py:116
  375.2 1.5 collective-permute-start.22
  376.8 7.0 collective-permute-start.23
  383.8 66.7 %copy-start.4 = (bf16[384,1536]{1,0:T(8,128)(2,1)S(1)}, bf16[384,1536]{1,0:T(8,128)(2,1)}, u32[]{:S(2)}) copy-start(bf16[384,1536]{1,0:T(8,128)(2,1)} %param.8) | copy-start | bytes 3538948
  383.8 59.0 %collective-permute-start.24 = (f32[32,1536]{1,0:T(8,128)S(1)}, f32[32,1536]{1,0:T(8,128)S(1)}, u32[]{:S(2)}, u32[]{:S(2)}) collective-permute-start(f32[32,1536]{1,0:T(8,128)S(1)} %add.429), channel_id=1, source_target_pairs={{0,4},{1,5},{2,6},{3,7},{4,0},{5,1},{6,2},{7,3},{8,12},{9,13},{10,... | collective-permute-start | bytes 589832 | tf_op jit(solution)/shard_map/ppermute | solution.py:22
  394.4 1.2 collective-permute-start.27
  394.5 1.7 collective-permute-start.32
  395.6 3.7 collective-permute-start.28
  396.2 3.7 collective-permute-start.33
  399.3 41.4 %collective-permute-start.29 = (f32[1536]{0:T(1024)S(1)}, f32[1536]{0:T(1024)S(1)}, u32[]{:S(2)}, u32[]{:S(2)}) collective-permute-start(f32[1536]{0:T(1024)S(1)} %add.434), channel_id=1, source_target_pairs={{0,4},{1,5},{2,6},{3,7},{4,0},{5,1},{6,2},{7,3},{8,12},{9,13},{10,... | collective-permute-start | bytes 18440 | tf_op jit(solution)/shard_map/ppermute | solution.py:22
  399.9 41.2 %collective-permute-start.34 = (f32[1536]{0:T(1024)S(1)}, f32[1536]{0:T(1024)S(1)}, u32[]{:S(2)}, u32[]{:S(2)}) collective-permute-start(f32[1536]{0:T(1024)S(1)} %add.439), channel_id=1, source_target_pairs={{0,4},{1,5},{2,6},{3,7},{4,0},{5,1},{6,2},{7,3},{8,12},{9,13},{10,... | collective-permute-start | bytes 18440 | tf_op jit(solution)/shard_map/ppermute | solution.py:22
  440.7 3.7 collective-permute-start.30
  441.1 3.7 collective-permute-start.35
  442.8 7.6 collective-permute-start.25
  444.4 7.9 collective-permute-start.31
  444.8 8.2 collective-permute-start.36
  450.5 15.4 %collective-permute-start.26 = (f32[32,1536]{1,0:T(8,128)S(1)}, f32[32,1536]{1,0:T(8,128)S(1)}, u32[]{:S(2)}, u32[]{:S(2)}) collective-permute-start(f32[32,1536]{1,0:T(8,128)S(1)} %add.431), channel_id=1, source_target_pairs={{0,16},{1,17},{2,18},{3,19},{4,20},{5,21},{6,22},{7,23},{8,24},{9,... | collective-permute-start | bytes 589832 | tf_op jit(solution)/shard_map/ppermute | solution.py:22
  (6 other events, 11.4 us)
Sparse Core Ops, SparseCore 0:
  9.6 66.9 all-gather.3
  228.1 140.8 reduce-scatter.1
  370.6 720.9 all-gather.5
